TPU v7x, 32 devices: a whole 2x2x4 slice. The times are simulated.
32 devices in a mesh: req: 4 (over y, x), mp: 8 (over z, core).
Axes of the slice: x: 2, y: 2, z: 4, core: 2. Of those that a mesh axis runs over, the one named last changes fastest.
Arguments:
- tokens: bfloat16 [1024, 2048], P('req'), may hold values from -6 to 6
- lengths: int32 [4, 8], P('req'), may hold values from 1 to 80, 256 in all within a row
- response: int32 [1024], P('req'), may hold values 0 or 1
- targets: int32 [1024], replicated, may hold values from 0 to 32063, as said below
- attn_gain: float32 [2, 2048], replicated, may hold values from 0.5 to 1.5
- w_query: bfloat16 [2, 2048, 2048], P(None, None, 'mp')
- w_key: bfloat16 [2, 2048, 512], replicated, may hold values from -0.125 to 0.125
- w_value: bfloat16 [2, 2048, 512], replicated, may hold values from -0.125 to 0.125
- output_weight: bfloat16 [2, 2048, 2048], P(None, 'mp'), may hold values from -0.125 to 0.125
- mlp_gain: float32 [2, 2048], replicated, may hold values from 0.5 to 1.5
- w_gate: bfloat16 [2, 2048, 8192], P(None, None, 'mp'), may hold values from -0.125 to 0.125
- w_up: bfloat16 [2, 2048, 8192], P(None, None, 'mp'), may hold values from -0.125 to 0.125
- w_down: bfloat16 [2, 8192, 2048], P(None, 'mp'), may hold values from -0.0625 to 0.0625
- final_gain: float32 [2, 2048], replicated, may hold values from 0.5 to 1.5
- w_head: bfloat16 [2, 2048, 32064], P(None, None, ('req', 'mp'))
Outputs:
- token_diff: float32 [1024], P(('req', 'mp'))
- request_sum: float32 [4, 8], P('req')
- request_peak: float32 [4, 8], P('req')
Inputs may be any that keep to these rules, and one draw needn't show every extreme that they name: `lengths`: each row sums to 256; some request of each tenant has exactly 80 tokens. `targets`: vocabulary ids.
All inputs are finite; a program needn't handle non-finite values. No bound on the sum of `response` on one device may be relied on, other than what follows from the above.
Results may differ from a plain program's by a relative error of at most 0.04.
Values may be sent and summed in bfloat16 or wider, within the bound.
No kernel may reach another device: no remote copies, remote signals or barrier semaphores. Data moves between devices by JAX's collectives and lax.ppermute only.
A program may use at most 128 MiB of HBM per device.

v0:
```python
import jax
import jax.numpy as jnp
from jax import lax
from jax.sharding import PartitionSpec as P

HEADS = 32
KV_HEADS = 8
HEAD_DIM = 64
epsilon = 1e-05
theta = 500000.0


def merged(part, axis, combine):
    gathered = jax.tree.map(lambda a: lax.all_gather(a, axis), part)

    def take(source):
        return jax.tree.map(lambda a: lax.dynamic_index_in_dim(a, source, 0, False), gathered)

    return lax.fori_loop(
        1, lax.axis_size(axis), lambda source, state: combine(state, take(source)), take(0)
    )


def rms_scale(entries, scaling):
    entries = entries.astype(jnp.float32)
    inverse = lax.rsqrt(jnp.mean(entries * entries, axis=-1, keepdims=True) + epsilon)
    return entries * inverse * scaling


def rotate(entries, positions):
    halfway = entries.shape[-1] // 2
    frequency = theta ** (-jnp.arange(halfway, dtype=jnp.float32) * 2.0 / entries.shape[-1])
    angles = positions.astype(jnp.float32)[:, None] * frequency[None, :]
    cosine = jnp.cos(angles)
    sine_part = jnp.sin(angles)
    former = entries[..., :halfway]
    latter = entries[..., halfway:]
    return jnp.concatenate(
        [former * cosine - latter * sine_part, latter * cosine + former * sine_part], axis=-1
    )


def request_layout(length_row, slot_count):
    end_slot = jnp.cumsum(length_row, dtype=jnp.int32)
    start_slot = end_slot - length_row
    slot_ids = jnp.arange(slot_count, dtype=jnp.int32)
    member = (slot_ids[:, None] >= start_slot[None, :]) & (slot_ids[:, None] < end_slot[None, :])
    segment = jnp.sum((slot_ids[:, None] >= end_slot[None, :]).astype(jnp.int32), axis=1)
    offset = jnp.sum(jnp.where(member, start_slot[None, :], 0), axis=1)
    return (member, segment, slot_ids - offset)


def allowed_pairs(segment):
    slot_ids = jnp.arange(segment.shape[0], dtype=jnp.int32)
    return (segment[:, None] == segment[None, :]) & (slot_ids[None, :] <= slot_ids[:, None])


def attend_heads(query, key_rows, value_rows, positions, allowed, repeat_times):
    slot_count = query.shape[0]
    query = rotate(query.reshape(slot_count, -1, HEAD_DIM).transpose(1, 0, 2), positions).astype(
        jnp.bfloat16
    )
    key_rows = rotate(
        key_rows.reshape(slot_count, -1, HEAD_DIM).transpose(1, 0, 2), positions
    ).astype(jnp.bfloat16)
    value_rows = (
        value_rows.reshape(slot_count, -1, HEAD_DIM).transpose(1, 0, 2).astype(jnp.bfloat16)
    )
    key_rows = jnp.repeat(key_rows, repeat_times, axis=0)
    value_rows = jnp.repeat(value_rows, repeat_times, axis=0)
    scores = jnp.einsum(
        "hqd,hkd->hqk", query.astype(jnp.float32), key_rows.astype(jnp.float32)
    ) * HEAD_DIM ** (-0.5)
    scores = jnp.where(allowed[None], scores, -1e30)
    highest = jnp.max(scores, axis=-1, keepdims=True)
    weights = jnp.exp(scores - highest)
    probs = (weights / jnp.sum(weights, axis=-1, keepdims=True)).astype(jnp.bfloat16)
    attended = jnp.einsum(
        "hqk,hkd->hqd", probs.astype(jnp.float32), value_rows.astype(jnp.float32)
    ).astype(jnp.bfloat16)
    return attended.transpose(1, 0, 2).reshape(slot_count, -1)


def per_device(
    tokens,
    lengths,
    response,
    targets,
    attn_gain,
    w_query,
    w_key,
    w_value,
    output_weight,
    mlp_gain,
    w_gate,
    w_up,
    w_down,
    final_gain,
    w_head,
):
    group_rows = tokens.shape[0]
    own_rows = group_rows // lax.axis_size("mp")
    mp_index = lax.axis_index("mp")
    member, segment, positions = request_layout(lengths[0], group_rows)
    allowed = allowed_pairs(segment)
    heads_here = w_query.shape[2] // HEAD_DIM
    sharing = HEADS // KV_HEADS
    kv_here = max(1, heads_here // sharing)
    kv_first = mp_index * heads_here // sharing * HEAD_DIM
    key_cols = lax.dynamic_slice_in_dim(w_key, kv_first, kv_here * HEAD_DIM, 2)
    value_columns = lax.dynamic_slice_in_dim(w_value, kv_first, kv_here * HEAD_DIM, 2)
    attended_list = []
    for model in range(2):
        normed = rms_scale(tokens, attn_gain[model]).astype(jnp.bfloat16)
        query = jnp.dot(normed, w_query[model], preferred_element_type=jnp.float32)
        keys_here = jnp.dot(normed, key_cols[model], preferred_element_type=jnp.float32)
        values_here = jnp.dot(normed, value_columns[model], preferred_element_type=jnp.float32)
        attended_list.append(
            attend_heads(
                query, keys_here, values_here, positions, allowed, min(sharing, heads_here)
            )
        )
    attended = jnp.stack(attended_list, axis=1)
    selected_rows = attended
    mixed = lax.psum_scatter(
        jnp.einsum(
            "kbq,bqo->kbo", selected_rows, output_weight, preferred_element_type=jnp.float32
        ),
        "mp",
        scatter_dimension=0,
        tiled=True,
    )
    own_tokens = lax.dynamic_slice_in_dim(tokens, mp_index * own_rows, own_rows, 0)
    residual = own_tokens.astype(jnp.float32)[:, None, :] + mixed
    normed_mid = rms_scale(residual, mlp_gain).astype(jnp.bfloat16)
    row_block = lax.all_gather(normed_mid, "mp", axis=0, tiled=True)
    gate_part = jnp.einsum("nmd,mdf->nmf", row_block, w_gate, preferred_element_type=jnp.float32)
    lift_part = jnp.einsum("nmd,mdf->nmf", row_block, w_up, preferred_element_type=jnp.float32)
    hidden = (jax.nn.silu(gate_part) * lift_part).astype(jnp.bfloat16)
    selected_rows = hidden
    final = residual + lax.psum_scatter(
        jnp.einsum("nmf,mfd->nmd", selected_rows, w_down, preferred_element_type=jnp.float32),
        "mp",
        scatter_dimension=0,
        tiled=True,
    )
    closing = rms_scale(final, final_gain).astype(jnp.bfloat16)
    vocab_here = w_head.shape[2]
    vocab_first = lax.axis_index(("req", "mp")) * vocab_here
    column_ids = jnp.arange(vocab_here, dtype=jnp.int32)
    logits = jnp.einsum(
        "nmd,mdv->mnv",
        lax.all_gather(closing, ("req", "mp"), axis=0, tiled=True),
        w_head,
        preferred_element_type=jnp.float32,
    )
    peak_part = jnp.max(logits, axis=-1)
    total_part = jnp.sum(jnp.exp(logits - peak_part[..., None]), axis=-1)
    wanted = targets - vocab_first
    hit_part = jnp.sum(
        jnp.where(column_ids[None, None, :] == wanted[None, :, None], logits, 0.0), axis=-1
    )

    def join(first_stats, second_stats):
        peak_one, total_one, hit_one = first_stats
        peak_two, total_two, hit_two = second_stats
        highest = jnp.maximum(peak_one, peak_two)
        return (
            highest,
            total_one * jnp.exp(peak_one - highest) + total_two * jnp.exp(peak_two - highest),
            hit_one + hit_two,
        )

    peak_all, total_all, hit_all = merged((peak_part, total_part, hit_part), ("req", "mp"), join)
    log_likelihood = hit_all - (peak_all + jnp.log(total_all))
    gap = log_likelihood[0] - log_likelihood[1]
    group_gap = lax.dynamic_slice_in_dim(
        gap, lax.axis_index("req") * group_rows, group_rows, 0
    ) * response.astype(jnp.float32)
    token_out = lax.dynamic_slice_in_dim(group_gap, mp_index * own_rows, own_rows, 0)
    member_weights = member.astype(jnp.float32)
    request_sum = jnp.dot(group_gap, member_weights, precision=lax.Precision.HIGHEST)
    request_peak = jnp.max(member_weights * jnp.abs(group_gap)[:, None], axis=0)
    return (token_out, request_sum[None, :], request_peak[None, :])


def solution(mesh):
    placed = (
        P("req", None),
        P("req", None),
        P("req"),
        P(),
        P(),
        P(None, None, "mp"),
        P(),
        P(),
        P(None, "mp", None),
        P(),
        P(None, None, "mp"),
        P(None, None, "mp"),
        P(None, "mp", None),
        P(),
        P(None, None, ("req", "mp")),
    )
    return jax.shard_map(
        per_device,
        mesh=mesh,
        in_specs=placed,
        out_specs=(P(("req", "mp")), P("req", None), P("req", None)),
        check_vma=False,
    )
```

profile of v0, /device:TPU:0, one launch (start us, length us, event | category | flops | bytes accessed | tf_op | source)
XLA Modules:
  0.0 424.3 jit_solution(8450373626498625544)
XLA Ops:
  7.8 1.6 fusion.10
  11.8 2.7 slice_bitcast_fusion.1
  14.4 2.3 copy.34
  16.7 2.2 convolution_bitcast_fusion.5
  18.9 2.1 convolution_bitcast_fusion.4
  21.0 1.2 convolution_bitcast_fusion.2
  22.2 1.4 copy.32
  23.7 2.1 convolution_bitcast_fusion.3
  27.1 1.4 fusion.20
  29.0 1.3 fusion.19
  30.3 1.1 fusion.100
  31.5 1.7 convolution_convert_fusion.3
  33.2 2.3 convolution_convert_fusion.2
  35.6 2.0 convolution_convert_fusion.1
  37.7 1.9 convolution_convert_fusion
  39.8 2.6 convolution_bitcast_fusion.1
  42.6 52.7 %reduce-scatter.3.cloned.1.call-done = f32[32,2,2048]{2,0,1:T(8,128)} async-done(((f32[256,2,2048]{2,0,1:T(8,128)}), f32[32,2,2048]{2,0,1:T(8,128)}) %reduce-scatter.3.cloned.1.call-update) | async-done | bytes 524304 | tf_op jit(solution)/shard_map/reduce_scatter | solution.py:125
  95.3 1.2 multiply_reduce_fusion.1
  96.5 1.9 multiply_convert_fusion.1
  98.6 27.6 %all-gather.9.cloned.1.call-done = bf16[256,2,2048]{2,0,1:T(8,128)(2,1)} async-done(((bf16[32,2,2048]{2,0,1:T(8,128)(2,1)}), bf16[256,2,2048]{2,0,1:T(8,128)(2,1)}) %all-gather.9.cloned.1.call-update) | async-done | bytes 2097168 | tf_op jit(solution)/shard_map/all_gather | solution.py:136
  126.2 7.8 %fusion.111 = f32[2,256,1024]{2,1,0:T(8,128)} fusion(bf16[256,2,2048]{2,0,1:T(8,128)(2,1)} %all-gather.9.cloned.1.call-done, bf16[2,2048,1024]{2,1,0:T(8,128)(2,1)} %param.27), kind=kOutput, calls=%fused_computation.157 | convolution fusion | flops 2147483648 | bytes 12582912 | tf_op jit(solution)/shard_map/nmd,mdf->nmf/dot_general | solution.py:137
  134.0 13.1 %convolution_bitcast_fusion = f32[256,2,2048]{2,0,1:T(8,128)} fusion(bf16[2,1024,2048]{2,1,0:T(8,128)(2,1)} %param.29, f32[2,256,1024]{2,1,0:T(8,128)} %fusion.111, bf16[256,2,2048]{2,0,1:T(8,128)(2,1)S(1)} %copy-done.2, bf16[2,2048,1024]{2,1,0:T(8,128)(2,1)} %param.28), kind=kOutput, calls=%fused_computation.13 | convolution fusion | flops 4298113024 | bytes 25165824 | tf_op jit(solution)/shard_map/nmf,mfd->nmd/dot_general | solution.py:142
  147.4 49.2 %reduce-scatter.5.cloned.1.call-done = f32[32,2,2048]{2,0,1:T(8,128)} async-done(((f32[256,2,2048]{2,0,1:T(8,128)}), f32[32,2,2048]{2,0,1:T(8,128)}) %reduce-scatter.5.cloned.1.call-update) | async-done | bytes 524304 | tf_op jit(solution)/shard_map/reduce_scatter | solution.py:141
  196.6 1.2 multiply_reduce_fusion
  197.8 1.9 multiply_convert_fusion
  200.5 75.1 %all-gather.11.cloned.1.call-done = bf16[1024,2,2048]{2,0,1:T(8,128)(2,1)} async-done(((bf16[32,2,2048]{2,0,1:T(8,128)(2,1)}), bf16[1024,2,2048]{2,0,1:T(8,128)(2,1)}) %all-gather.11.cloned.1.call-update) | async-done | bytes 8388624 | tf_op jit(solution)/shard_map/all_gather | solution.py:153
  275.6 16.9 %fusion.110 = (f32[2,1024]{1,0:T(2,128)S(1)}, f32[2,1024,1002]{1,2,0:T(8,128)}) fusion(bf16[1024,2,2048]{2,0,1:T(8,128)(2,1)} %all-gather.11.cloned.1.call-done, bf16[2,2048,1002]{1,0,2:T(2,128)(2,1)} %param.31), kind=kOutput, calls=%fused_computation.156 | convolution fusion | flops 8407435264 | bytes 24813568 | tf_op jit(solution)/shard_map/nmd,mdv->mnv/dot_general | solution.py:151
  292.5 4.6 %select_reduce_fusion = (f32[2,1024]{1,0:T(2,128)S(1)}, f32[2,1024]{1,0:T(2,128)S(1)}) fusion(f32[2,1024,1002]{1,2,0:T(8,128)} %get-tuple-element.228, pred[1024,1002]{0,1:T(8,128)(4,1)S(1)} %iota_compare_fusion, f32[2,1024]{1,0:T(2,128)S(1)} %get-tuple-element.227), kind=kLoop, calls=%fused_computation.10 | loop fusion | flops 8204288 | bytes 9259008 | tf_op jit(solution)/shard_map/reduce_sum | solution.py:160
  297.1 40.2 %all-gather.5 = f32[32,2,1024]{2,1,0:T(2,128)S(1)} all-gather(f32[1,2,1024]{2,1,0:T(2,128)S(1)} %bitcast.132), channel_id=4, replica_groups=mesh['req'=4,'mp'=8] {'req','mp'}, dimensions={0}, use_global_device_ids=true | all-gather | bytes 270336 | tf_op jit(solution)/shard_map/all_gather | solution.py:14
  337.3 37.7 %all-gather.4 = f32[32,2,1024]{2,1,0:T(2,128)S(1)} all-gather(f32[1,2,1024]{2,1,0:T(2,128)S(1)} %bitcast.131), channel_id=3, replica_groups=mesh['req'=4,'mp'=8] {'req','mp'}, dimensions={0}, use_global_device_ids=true | all-gather | bytes 270336 | tf_op jit(solution)/shard_map/all_gather | solution.py:14
  374.9 39.0 %all-gather.3 = f32[32,2,1024]{2,1,0:T(2,128)S(1)} all-gather(f32[1,2,1024]{2,1,0:T(2,128)S(1)} %bitcast.130), channel_id=2, replica_groups=mesh['req'=4,'mp'=8] {'req','mp'}, dimensions={0}, use_global_device_ids=true | all-gather | bytes 270336 | tf_op jit(solution)/shard_map/all_gather | solution.py:14
  413.9 1.7 while.19
  (113 shorter events, 9.6 us)
Async XLA Ops:
  7.2 32.6 %copy-start = (bf16[2,256,2048]{2,1,0:T(8,128)(2,1)S(1)}, bf16[2,256,2048]{2,1,0:T(8,128)(2,1)}, u32[]{:S(2)}) copy-start(bf16[2,256,2048]{2,1,0:T(8,128)(2,1)} %param.25) | copy-start | bytes 6291460
  7.2 88.1 %reduce-scatter.3.cloned.1.call-start = ((), (), s32[]{:S(2)}) async-start(), calls=%async_computation.2 | async-start | bytes 4718592 | tf_op jit(solution)/shard_map/reduce_scatter | solution.py:125
  9.3 9.6 %copy-start.18 = (f32[256]{0:T(256)}, f32[256]{0:T(256)S(1)}, u32[]{:S(2)}) copy-start(f32[256]{0:T(256)S(1)} %add_rsqrt_fusion.2) | copy-start | bytes 3076
  10.1 6.6 %copy-start.10 = (f32[1,2048]{1,0:T(1,128)}, f32[1,2048]{1,0:T(1,128)S(1)}, u32[]{:S(2)}) copy-start(f32[1,2048]{1,0:T(1,128)S(1)} %get-tuple-element.219) | copy-start | bytes 24580
  11.0 3.4 copy-start.14
  11.7 2.8 copy-start.16
  16.7 4.3 %copy-start.4 = (bf16[256,2048]{1,0:T(8,128)(2,1)S(1)}, bf16[256,2048]{1,0:T(8,128)(2,1)}, u32[]{:S(2)}) copy-start(bf16[256,2048]{1,0:T(8,128)(2,1)} %param.17) | copy-start | bytes 3145732
  16.7 4.3 %copy-start.6 = (bf16[256,2048]{1,0:T(8,128)(2,1)S(1)}, bf16[256,2048]{1,0:T(8,128)(2,1)}, u32[]{:S(2)}) copy-start(bf16[256,2048]{1,0:T(8,128)(2,1)} %copy.34) | copy-start | bytes 3145732
  23.7 2.3 copy-start.13
  27.0 2.0 copy-start.7
  29.0 2.5 copy-start.5
  29.0 2.5 copy-start.11
  29.0 2.5 copy-start.19
  35.6 2.2 copy-start.21
  42.4 54.0 %copy-start.8 = (f32[2,2048]{1,0:T(2,128)S(1)}, f32[2,2048]{1,0:T(2,128)}, u32[]{:S(2)}) copy-start(f32[2,2048]{1,0:T(2,128)} %param.26) | copy-start | bytes 49156
  42.5 83.7 %all-gather.9.cloned.1.call-start = ((), (), s32[]{:S(2)}) async-start(), calls=%async_computation.3 | async-start | bytes 2359296 | tf_op jit(solution)/shard_map/all_gather | solution.py:136
  98.4 98.2 %reduce-scatter.5.cloned.1.call-start = ((), (), s32[]{:S(2)}) async-start(), calls=%async_computation.4 | async-start | bytes 4718592 | tf_op jit(solution)/shard_map/reduce_scatter | solution.py:141
  126.2 7.8 %copy-start.2 = (bf16[256,2,2048]{2,0,1:T(8,128)(2,1)S(1)}, bf16[256,2,2048]{2,0,1:T(8,128)(2,1)}, u32[]{:S(2)}) copy-start(bf16[256,2,2048]{2,0,1:T(8,128)(2,1)} %all-gather.9.cloned.1.call-done) | copy-start | bytes 6291460
  147.1 49.5 %copy-start.3 = (f32[32,2,2048]{2,0,1:T(8,128)S(1)}, f32[32,2,2048]{2,0,1:T(8,128)}, u32[]{:S(2)}) copy-start(f32[32,2,2048]{2,0,1:T(8,128)} %reduce-scatter.3.cloned.1.call-done) | copy-start | bytes 1572868
  147.1 50.7 %copy-start.9 = (f32[2,2048]{1,0:T(2,128)S(1)}, f32[2,2048]{1,0:T(2,128)}, u32[]{:S(2)}) copy-start(f32[2,2048]{1,0:T(2,128)} %param.30) | copy-start | bytes 49156
  147.1 52.6 %copy-start.12 = (s32[1024]{0:T(1024)S(1)}, s32[1024]{0:T(1024)}, u32[]{:S(2)}) copy-start(s32[1024]{0:T(1024)} %param.20) | copy-start | bytes 12292
  147.1 128.5 %all-gather.11.cloned.1.call-start = ((), (), s32[]{:S(2)}) async-start(), calls=%async_computation.5 | async-start | bytes 8650752 | tf_op jit(solution)/shard_map/all_gather | solution.py:153
  292.5 123.3 %copy-start.20 = (s32[256]{0:T(256)S(1)}, s32[256]{0:T(256)}, u32[]{:S(2)}) copy-start(s32[256]{0:T(256)} %param.19) | copy-start | bytes 3076
  292.5 123.3 %copy-start.15 = (s32[8,1]{0,1:T(1,128)S(1)}, s32[8,1]{0,1:T(1,128)}, u32[]{:S(2)}) copy-start(s32[8,1]{0,1:T(1,128)} %copy-done.14) | copy-start | bytes 100
  292.5 123.3 %copy-start.17 = (s32[8]{0:T(128)S(1)}, s32[8]{0:T(128)}, u32[]{:S(2)}) copy-start(s32[8]{0:T(128)} %copy-done.16) | copy-start | bytes 100
  292.5 125.3 %copy-start.1 = (bf16[2,256,2048]{2,1,0:T(8,128)(2,1)S(1)}, bf16[2,256,2048]{2,1,0:T(8,128)(2,1)}, u32[]{:S(2)}) copy-start(bf16[2,256,2048]{2,1,0:T(8,128)(2,1)} %param.25) | copy-start | bytes 6291460
Sparse Core Ops, SparseCore 0:
  42.6 52.6 reduce-scatter.2
  98.5 27.6 all-gather.8
  147.3 49.3 reduce-scatter.4
  199.8 75.7 all-gather.10
where the time goes:
time: 425 us; the launch traced here: 424 us
  waiting for transfers between devices  205 us (48%)
  blocking collectives  117 us (28%)
  matrix products  61.2 us (14%)
  other arithmetic  18.2 us (4%)
  between operations  14.1 us (3%)
  local copies, waits for them, and re-layouts  8.11 us (2%)
    all_gather x3, blocking collectives, merged(): gathered = jax.tree.map(lambda a: lax.all_gather(a, axis), part)  117 us
    all_gather x1, waiting for transfers between devices, per_device(): lax.all_gather(closing, ('req', 'mp'), axis=0, tiled=True)  75.1 us
    reduce_scatter x1, waiting for transfers between devices, per_device(): lax.psum_scatter(jnp.einsum('kbq,bqo->kbo', selected_rows, output_weight,...  52.7 us
    reduce_scatter x1, waiting for transfers between devices, per_device(): lax.psum_scatter(jnp.einsum('nmf,mfd->nmd', selected_rows, w_down, prefer...  49.2 us
    all_gather x1, waiting for transfers between devices, per_device(): row_block = lax.all_gather(normed_mid, 'mp', axis=0, tiled=True)  27.6 us
    dot_general x1, matrix products, per_device(): jnp.einsum('nmd,mdv->mnv', lax.all_gather(closing, ('req', 'mp'), axis=0,...  16.9 us
    dot_general x1, matrix products, per_device(): jnp.einsum('nmf,mfd->nmd', selected_rows, w_down, preferred_element_type=...  13.1 us
  transfers between devices with their start and end apart: 4, of which 4 were waited for; matrix products, arithmetic and copies ran while one was open for 0% of the time, Pallas kernels for 0%

commit v1 on v0

--- a/solution.py
+++ b/solution.py
@@ -133,7 +133,16 @@
     own_tokens = lax.dynamic_slice_in_dim(tokens, mp_index * own_rows, own_rows, 0)
     residual = own_tokens.astype(jnp.float32)[:, None, :] + mixed
     normed_mid = rms_scale(residual, mlp_gain).astype(jnp.bfloat16)
-    row_block = lax.all_gather(normed_mid, "mp", axis=0, tiled=True)
+    ways = lax.axis_size("mp")
+    up = [(d, (d + 1) % ways) for d in range(ways)]
+    down = [(d, (d - 1) % ways) for d in range(ways)]
+    earlier, later = ([normed_mid], [normed_mid])
+    for _ in range(ways // 2):
+        earlier.append(lax.ppermute(earlier[-1], "mp", up))
+    for _ in range((ways - 1) // 2):
+        later.append(lax.ppermute(later[-1], "mp", down))
+    line = jnp.concatenate([*earlier[::-1], *later[1:]], axis=0)
+    row_block = jnp.roll(line, (lax.axis_index("mp") - ways // 2) * normed_mid.shape[0], axis=0)
     gate_part = jnp.einsum("nmd,mdf->nmf", row_block, w_gate, preferred_element_type=jnp.float32)
     lift_part = jnp.einsum("nmd,mdf->nmf", row_block, w_up, preferred_element_type=jnp.float32)
     hidden = (jax.nn.silu(gate_part) * lift_part).astype(jnp.bfloat16)

time: 425 us -> 438 us (1.031)
  starting transfers between devices: 0.56 us -> 11.5 us
  waiting for transfers between devices: 205 us -> 199 us
    all_gather x1 -> x0, waiting for transfers between devices: 27.6 us -> none  [per_device(): row_block = lax.all_gather(normed_mid, 'mp', axis=0, tiled=True)]
    ppermute x0 -> x7, waiting for transfers between devices: none -> 19.9 us  [the longest x4 19.8 us: per_device(): earlier.append(lax.ppermute(earlier[-1], 'mp', up))]
    ppermute x0 -> x7, starting transfers between devices: none -> 11.1 us  [the longest x3 11.1 us: per_device(): later.append(lax.ppermute(later[-1], 'mp', down))]
  transfers between devices with their start and end apart: 4 -> 10, of which waited for: 4 -> 7; matrix products, arithmetic and copies ran while one was open for 0% -> 0% of each run, Pallas kernels for 0% -> 0%
where the time goes in v1:
time: 438 us; the launch traced here: 437 us
  waiting for transfers between devices  199 us (45%)
  blocking collectives  117 us (27%)
  matrix products  64.1 us (15%)
  other arithmetic  19.9 us (5%)
  between operations  14.2 us (3%)
  starting transfers between devices  11.5 us (3%)
  local copies, waits for them, and re-layouts  11 us (3%)
    all_gather x3, blocking collectives, merged(): gathered = jax.tree.map(lambda a: lax.all_gather(a, axis), part)  117 us
    all_gather x1, waiting for transfers between devices, per_device(): lax.all_gather(closing, ('req', 'mp'), axis=0, tiled=True)  75.1 us
    reduce_scatter x1, waiting for transfers between devices, per_device(): lax.psum_scatter(jnp.einsum('kbq,bqo->kbo', selected_rows, output_weight,...  52.7 us
    reduce_scatter x1, waiting for transfers between devices, per_device(): lax.psum_scatter(jnp.einsum('nmf,mfd->nmd', selected_rows, w_down, prefer...  51.3 us
    ppermute x4, waiting for transfers between devices, per_device(): earlier.append(lax.ppermute(earlier[-1], 'mp', up))  19.8 us
    dot_general x1, matrix products, per_device(): jnp.einsum('nmd,mdv->mnv', lax.all_gather(closing, ('req', 'mp'), axis=0,...  16.9 us
    dot_general x1, matrix products, per_device(): jnp.einsum('nmf,mfd->nmd', selected_rows, w_down, preferred_element_type=...  13.7 us
    ppermute x3, starting transfers between devices, per_device(): later.append(lax.ppermute(later[-1], 'mp', down))  11.1 us
  transfers between devices with their start and end apart: 10, of which 7 were waited for; matrix products, arithmetic and copies ran while one was open for 0% of the time, Pallas kernels for 0%

profile of v1, /device:TPU:0, one launch (start us, length us, event | category | flops | bytes accessed | tf_op | source)
XLA Modules:
  0.0 437.3 jit_solution(4345024054863517348)
XLA Ops:
  11.8 2.7 slice_bitcast_fusion.1
  14.5 2.3 copy.34
  16.7 2.0 convolution_bitcast_fusion.5
  18.8 2.7 convolution_bitcast_fusion.4
  21.5 2.1 convolution_bitcast_fusion.2
  25.0 2.1 convolution_bitcast_fusion.3
  33.9 2.2 fusion.27
  37.3 1.7 convolution_convert_fusion.3
  39.0 2.3 convolution_convert_fusion.2
  41.4 1.9 convolution_convert_fusion.1
  43.4 2.0 convolution_convert_fusion
  45.6 2.6 convolution_bitcast_fusion.1
  48.3 52.7 %reduce-scatter.3.cloned.1.call-done = f32[32,2,2048]{2,0,1:T(8,128)} async-done(((f32[256,2,2048]{2,0,1:T(8,128)}), f32[32,2,2048]{2,0,1:T(8,128)}) %reduce-scatter.3.cloned.1.call-update) | async-done | bytes 524304 | tf_op jit(solution)/shard_map/reduce_scatter | solution.py:125
  103.5 7.6 %collective-permute-done = bf16[32,2,2048]{2,0,1:T(8,128)(2,1)S(1)} collective-permute-done((bf16[32,2,2048]{2,0,1:T(8,128)(2,1)S(1)}, bf16[32,2,2048]{2,0,1:T(8,128)(2,1)S(1)}, u32[]{:S(2)}, u32[]{:S(2)}) %collective-permute-start) | collective-permute-done | bytes 262176 | tf_op jit(solution)/shard_map/ppermute | solution.py:141
  111.2 3.5 collective-permute-start.4
  114.7 4.5 %collective-permute-done.1 = bf16[32,2,2048]{2,0,1:T(8,128)(2,1)S(1)} collective-permute-done((bf16[32,2,2048]{2,0,1:T(8,128)(2,1)S(1)}, bf16[32,2,2048]{2,0,1:T(8,128)(2,1)S(1)}, u32[]{:S(2)}, u32[]{:S(2)}) %collective-permute-start.1) | collective-permute-done | bytes 262176 | tf_op jit(solution)/shard_map/ppermute | solution.py:141
  119.2 3.8 collective-permute-start.5
  123.0 3.9 collective-permute-done.2
  126.9 3.8 collective-permute-start.6
  130.7 3.8 collective-permute-done.3
  135.2 2.0 copy-done.11
  137.1 7.1 %fusion.17 = f32[2,256,1024]{2,1,0:T(8,128)} fusion(bf16[2,2048,1024]{2,1,0:T(8,128)(2,1)} %param.27, bf16[512,2,2048]{2,0,1:T(8,128)(2,1)S(1)} %constant_dynamic-update-slice_fusion, s32[]{:T(128)S(6)} %select_n.66), kind=kOutput, calls=%fused_computation.31 | convolution fusion | flops 2147483648 | bytes 12582916 | tf_op jit(solution)/shard_map/nmd,mdf->nmf/dot_general | solution.py:146
  144.2 13.7 %convolution_bitcast_fusion = f32[256,2,2048]{2,0,1:T(8,128)} fusion(bf16[2,1024,2048]{2,1,0:T(8,128)(2,1)} %param.29, f32[2,256,1024]{2,1,0:T(8,128)} %fusion.17, bf16[2,2048,1024]{2,1,0:T(8,128)(2,1)} %param.28, bf16[512,2,2048]{2,0,1:T(8,128)(2,1)} %copy-done.11, s32[]{:T(128)S(6)} %select_n.66), kind=kOutput, calls=%fused_computation.13 | convolution fusion | flops 4298113024 | bytes 25165828 | tf_op jit(solution)/shard_map/nmf,mfd->nmd/dot_general | solution.py:151
  158.2 51.3 %reduce-scatter.5.cloned.1.call-done = f32[32,2,2048]{2,0,1:T(8,128)} async-done(((f32[256,2,2048]{2,0,1:T(8,128)}), f32[32,2,2048]{2,0,1:T(8,128)}) %reduce-scatter.5.cloned.1.call-update) | async-done | bytes 524304 | tf_op jit(solution)/shard_map/reduce_scatter | solution.py:150
  210.8 1.9 multiply_convert_fusion
  213.4 75.1 %all-gather.8.cloned.1.call-done = bf16[1024,2,2048]{2,0,1:T(8,128)(2,1)} async-done(((bf16[32,2,2048]{2,0,1:T(8,128)(2,1)}), bf16[1024,2,2048]{2,0,1:T(8,128)(2,1)}) %all-gather.8.cloned.1.call-update) | async-done | bytes 8388624 | tf_op jit(solution)/shard_map/all_gather | solution.py:162
  288.5 16.9 %fusion.121 = (f32[2,1024]{1,0:T(2,128)S(1)}, f32[2,1024,1002]{1,2,0:T(8,128)}) fusion(bf16[1024,2,2048]{2,0,1:T(8,128)(2,1)} %all-gather.8.cloned.1.call-done, bf16[2,2048,1002]{1,0,2:T(2,128)(2,1)} %param.31), kind=kOutput, calls=%fused_computation.178 | convolution fusion | flops 8407435264 | bytes 24813568 | tf_op jit(solution)/shard_map/nmd,mdv->mnv/dot_general | solution.py:160
  305.4 4.6 %select_reduce_fusion = (f32[2,1024]{1,0:T(2,128)S(1)}, f32[2,1024]{1,0:T(2,128)S(1)}) fusion(f32[2,1024,1002]{1,2,0:T(8,128)} %get-tuple-element.228, pred[1024,1002]{0,1:T(8,128)(4,1)S(1)} %iota_compare_fusion, f32[2,1024]{1,0:T(2,128)S(1)} %get-tuple-element.227), kind=kLoop, calls=%fused_computation.10 | loop fusion | flops 8204288 | bytes 9259008 | tf_op jit(solution)/shard_map/reduce_sum | solution.py:169
  310.0 40.2 %all-gather.5 = f32[32,2,1024]{2,1,0:T(2,128)S(1)} all-gather(f32[1,2,1024]{2,1,0:T(2,128)S(1)} %bitcast.130), channel_id=4, replica_groups=mesh['req'=4,'mp'=8] {'req','mp'}, dimensions={0}, use_global_device_ids=true | all-gather | bytes 270336 | tf_op jit(solution)/shard_map/all_gather | solution.py:14
  350.2 37.7 %all-gather.4 = f32[32,2,1024]{2,1,0:T(2,128)S(1)} all-gather(f32[1,2,1024]{2,1,0:T(2,128)S(1)} %bitcast.129), channel_id=3, replica_groups=mesh['req'=4,'mp'=8] {'req','mp'}, dimensions={0}, use_global_device_ids=true | all-gather | bytes 270336 | tf_op jit(solution)/shard_map/all_gather | solution.py:14
  387.9 39.0 %all-gather.3 = f32[32,2,1024]{2,1,0:T(2,128)S(1)} all-gather(f32[1,2,1024]{2,1,0:T(2,128)S(1)} %bitcast.128), channel_id=2, replica_groups=mesh['req'=4,'mp'=8] {'req','mp'}, dimensions={0}, use_global_device_ids=true | all-gather | bytes 270336 | tf_op jit(solution)/shard_map/all_gather | solution.py:14
  426.9 1.7 while.19
  (142 shorter events, 22.6 us)
Async XLA Ops:
  7.2 38.4 %copy-start = (bf16[2,256,2048]{2,1,0:T(8,128)(2,1)S(1)}, bf16[2,256,2048]{2,1,0:T(8,128)(2,1)}, u32[]{:S(2)}) copy-start(bf16[2,256,2048]{2,1,0:T(8,128)(2,1)} %param.25) | copy-start | bytes 6291460
  7.2 93.9 %reduce-scatter.3.cloned.1.call-start = ((), (), s32[]{:S(2)}) async-start(), calls=%async_computation.2 | async-start | bytes 4718592 | tf_op jit(solution)/shard_map/reduce_scatter | solution.py:125
  9.3 15.7 %copy-start.19 = (f32[256]{0:T(256)}, f32[256]{0:T(256)S(1)}, u32[]{:S(2)}) copy-start(f32[256]{0:T(256)S(1)} %add_rsqrt_fusion.2) | copy-start | bytes 3076
  10.1 14.9 %copy-start.12 = (f32[1,2048]{1,0:T(1,128)}, f32[1,2048]{1,0:T(1,128)S(1)}, u32[]{:S(2)}) copy-start(f32[1,2048]{1,0:T(1,128)S(1)} %get-tuple-element.219) | copy-start | bytes 24580
  11.0 10.5 %copy-start.15 = (s32[8,1]{0,1:T(1,128)}, s32[8,1]{0,1:T(1,128)S(1)}, u32[]{:S(2)}) copy-start(s32[8,1]{0,1:T(1,128)S(1)} %reduce-window.4) | copy-start | bytes 100
  11.7 9.8 %copy-start.17 = (s32[8]{0:T(128)}, s32[8]{0:T(128)S(1)}, u32[]{:S(2)}) copy-start(s32[8]{0:T(128)S(1)} %fusion.87) | copy-start | bytes 100
  27.1 10.1 %copy-start.3 = (bf16[256,2048]{1,0:T(8,128)(2,1)S(1)}, bf16[256,2048]{1,0:T(8,128)(2,1)}, u32[]{:S(2)}) copy-start(bf16[256,2048]{1,0:T(8,128)(2,1)} %param.17) | copy-start | bytes 3145732
  29.2 8.1 %copy-start.13 = (f32[1,2048]{1,0:T(1,128)S(1)}, f32[1,2048]{1,0:T(1,128)}, u32[]{:S(2)}) copy-start(f32[1,2048]{1,0:T(1,128)} %copy-done.12) | copy-start | bytes 24580
  29.8 0.7 copy-start.9
  30.5 0.6 copy-start.6
  30.5 5.6 %copy-start.4 = (bf16[4,256,32]{1,2,0:T(8,128)(2,1)S(1)}, bf16[4,256,32]{1,2,0:T(8,128)(2,1)}, u32[]{:S(2)}) copy-start(bf16[4,256,32]{1,2,0:T(8,128)(2,1)} %get-tuple-element.218) | copy-start | bytes 196612
  30.5 5.6 %copy-start.8 = (bf16[256,64]{0,1:T(8,128)(2,1)S(1)}, bf16[256,64]{0,1:T(8,128)(2,1)}, u32[]{:S(2)}) copy-start(bf16[256,64]{0,1:T(8,128)(2,1)} %get-tuple-element.230) | copy-start | bytes 98308
  30.5 6.8 %copy-start.20 = (f32[256]{0:T(256)S(1)}, f32[256]{0:T(256)}, u32[]{:S(2)}) copy-start(f32[256]{0:T(256)} %copy-done.19) | copy-start | bytes 3076
  39.0 4.4 %copy-start.22 = (f32[4,256]{1,0:T(4,128)S(1)}, f32[4,256]{1,0:T(4,128)}, u32[]{:S(2)}) copy-start(f32[4,256]{1,0:T(4,128)} %fusion.111) | copy-start | bytes 12292
  48.2 54.1 %copy-start.7 = (f32[2,2048]{1,0:T(2,128)S(1)}, f32[2,2048]{1,0:T(2,128)}, u32[]{:S(2)}) copy-start(f32[2,2048]{1,0:T(2,128)} %param.26) | copy-start | bytes 49156
  48.2 161.3 %reduce-scatter.5.cloned.1.call-start = ((), (), s32[]{:S(2)}) async-start(), calls=%async_computation.3 | async-start | bytes 4718592 | tf_op jit(solution)/shard_map/reduce_scatter | solution.py:150
  101.0 33.6 %copy-start.2 = (f32[32,2,2048]{2,0,1:T(8,128)S(1)}, f32[32,2,2048]{2,0,1:T(8,128)}, u32[]{:S(2)}) copy-start(f32[32,2,2048]{2,0,1:T(8,128)} %reduce-scatter.3.cloned.1.call-done) | copy-start | bytes 1572868
  103.5 7.7 %collective-permute-start = (bf16[32,2,2048]{2,0,1:T(8,128)(2,1)S(1)}, bf16[32,2,2048]{2,0,1:T(8,128)(2,1)S(1)}, u32[]{:S(2)}, u32[]{:S(2)}) collective-permute-start(bf16[32,2,2048]{2,0,1:T(8,128)(2,1)S(1)} %multiply_convert_fusion.1), channel_id=1, source_target_pairs={{0,1},{1,2},{2,3},{3,4},{4,5},{5,6},{6,7},{7,0},{8,9},{9,10},{10,1... | collective-permute-start | bytes 786440 | tf_op jit(solution)/shard_map/ppermute | solution.py:141
  111.2 8.0 %collective-permute-start.1 = (bf16[32,2,2048]{2,0,1:T(8,128)(2,1)S(1)}, bf16[32,2,2048]{2,0,1:T(8,128)(2,1)S(1)}, u32[]{:S(2)}, u32[]{:S(2)}) collective-permute-start(bf16[32,2,2048]{2,0,1:T(8,128)(2,1)S(1)} %collective-permute-done), channel_id=1, source_target_pairs={{0,1},{1,2},{2,3},{3,4},{4,5},{5,6},{6,7},{7,0},{8,9},{9,10},{10,1... | collective-permute-start | bytes 786440 | tf_op jit(solution)/shard_map/ppermute | solution.py:141
  111.2 8.0 %collective-permute-start.4 = (bf16[32,2,2048]{2,0,1:T(8,128)(2,1)S(1)}, bf16[32,2,2048]{2,0,1:T(8,128)(2,1)S(1)}, u32[]{:S(2)}, u32[]{:S(2)}) collective-permute-start(bf16[32,2,2048]{2,0,1:T(8,128)(2,1)S(1)} %multiply_convert_fusion.1), channel_id=1, source_target_pairs={{0,7},{1,0},{2,1},{3,2},{4,3},{5,4},{6,5},{7,6},{8,15},{9,8},{10,9... | collective-permute-start | bytes 786440 | tf_op jit(solution)/shard_map/ppermute | solution.py:143
  119.2 7.7 %collective-permute-start.2 = (bf16[32,2,2048]{2,0,1:T(8,128)(2,1)S(1)}, bf16[32,2,2048]{2,0,1:T(8,128)(2,1)S(1)}, u32[]{:S(2)}, u32[]{:S(2)}) collective-permute-start(bf16[32,2,2048]{2,0,1:T(8,128)(2,1)S(1)} %collective-permute-done.1), channel_id=1, source_target_pairs={{0,1},{1,2},{2,3},{3,4},{4,5},{5,6},{6,7},{7,0},{8,9},{9,10},{10,1... | collective-permute-start | bytes 786440 | tf_op jit(solution)/shard_map/ppermute | solution.py:141
  119.2 7.7 %collective-permute-start.5 = (bf16[32,2,2048]{2,0,1:T(8,128)(2,1)S(1)}, bf16[32,2,2048]{2,0,1:T(8,128)(2,1)S(1)}, u32[]{:S(2)}, u32[]{:S(2)}) collective-permute-start(bf16[32,2,2048]{2,0,1:T(8,128)(2,1)S(1)} %collective-permute-done.4), channel_id=1, source_target_pairs={{0,7},{1,0},{2,1},{3,2},{4,3},{5,4},{6,5},{7,6},{8,15},{9,8},{10,9... | collective-permute-start | bytes 786440 | tf_op jit(solution)/shard_map/ppermute | solution.py:143
  126.9 7.6 %collective-permute-start.3 = (bf16[32,2,2048]{2,0,1:T(8,128)(2,1)S(1)}, bf16[32,2,2048]{2,0,1:T(8,128)(2,1)S(1)}, u32[]{:S(2)}, u32[]{:S(2)}) collective-permute-start(bf16[32,2,2048]{2,0,1:T(8,128)(2,1)S(1)} %collective-permute-done.2), channel_id=1, source_target_pairs={{0,1},{1,2},{2,3},{3,4},{4,5},{5,6},{6,7},{7,0},{8,9},{9,10},{10,1... | collective-permute-start | bytes 786440 | tf_op jit(solution)/shard_map/ppermute | solution.py:141
  126.9 7.9 %collective-permute-start.6 = (bf16[32,2,2048]{2,0,1:T(8,128)(2,1)S(1)}, bf16[32,2,2048]{2,0,1:T(8,128)(2,1)S(1)}, u32[]{:S(2)}, u32[]{:S(2)}) collective-permute-start(bf16[32,2,2048]{2,0,1:T(8,128)(2,1)S(1)} %collective-permute-done.5), channel_id=1, source_target_pairs={{0,7},{1,0},{2,1},{3,2},{4,3},{5,4},{6,5},{7,6},{8,15},{9,8},{10,9... | collective-permute-start | bytes 786440 | tf_op jit(solution)/shard_map/ppermute | solution.py:143
  135.1 2.0 copy-start.11
  157.9 52.8 %copy-start.10 = (f32[2,2048]{1,0:T(2,128)S(1)}, f32[2,2048]{1,0:T(2,128)}, u32[]{:S(2)}) copy-start(f32[2,2048]{1,0:T(2,128)} %param.30) | copy-start | bytes 49156
  157.9 54.7 %copy-start.14 = (s32[1024]{0:T(1024)S(1)}, s32[1024]{0:T(1024)}, u32[]{:S(2)}) copy-start(s32[1024]{0:T(1024)} %param.20) | copy-start | bytes 12292
  157.9 130.6 %all-gather.8.cloned.1.call-start = ((), (), s32[]{:S(2)}) async-start(), calls=%async_computation.4 | async-start | bytes 8650752 | tf_op jit(solution)/shard_map/all_gather | solution.py:162
  305.4 125.3 %copy-start.1 = (bf16[2,256,2048]{2,1,0:T(8,128)(2,1)S(1)}, bf16[2,256,2048]{2,1,0:T(8,128)(2,1)}, u32[]{:S(2)}) copy-start(bf16[2,256,2048]{2,1,0:T(8,128)(2,1)} %param.25) | copy-start | bytes 6291460
  305.4 123.3 %copy-start.21 = (s32[256]{0:T(256)S(1)}, s32[256]{0:T(256)}, u32[]{:S(2)}) copy-start(s32[256]{0:T(256)} %param.19) | copy-start | bytes 3076
  305.4 123.3 %copy-start.16 = (s32[8,1]{0,1:T(1,128)S(1)}, s32[8,1]{0,1:T(1,128)}, u32[]{:S(2)}) copy-start(s32[8,1]{0,1:T(1,128)} %copy-done.15) | copy-start | bytes 100
  305.4 123.3 %copy-start.18 = (s32[8]{0:T(128)S(1)}, s32[8]{0:T(128)}, u32[]{:S(2)}) copy-start(s32[8]{0:T(128)} %copy-done.17) | copy-start | bytes 100
  (1 other events, 0.6 us)
Sparse Core Ops, SparseCore 0:
  48.4 52.6 reduce-scatter.2
  158.1 51.4 reduce-scatter.4
  212.8 75.7 all-gather.7
